TPU v7x, 128 devices: a whole 4x4x4 slice. The times are simulated.
128 devices in a mesh: prow: 8 (over x, y_lo), pcol: 16 (over z, y_hi, core).
Axes of the slice: x: 4, y: 4 (y_hi: 2, y_lo: 2; y = y_hi * 2 + y_lo), z: 4, core: 2. Of those that a mesh axis runs over, the one named last changes fastest.
Arguments:
- trailing: bfloat16 [16384, 16384], P('prow', 'pcol'), may hold values from -6 to 6
- lower_slot_blocks: bfloat16 [16, 8192, 128], P('pcol', 'prow'), may hold values from -6 to 6
- l_rows: int32 [16, 64], P(None, 'prow'), may hold values from -1 to 127, as said below
- d_inv: bfloat16 [16, 128, 128], P('pcol'), may hold values from -0.5 to 0.5
- u_panel: bfloat16 [2048, 16384], P('prow', 'pcol'), may hold values from -0.125 to 0.125
- pivot: int32 [16, 128], P('prow'), may hold values from 0 to 127, each once within a row
Outputs:
- schur: bfloat16 [16384, 16384], P('prow', 'pcol')
Inputs may be any that keep to these rules, and one draw needn't show every extreme that they name: `l_rows`: for each panel, the entries are taken in aligned groups of 8, group g belonging to block rows g * 16 to (g + 1) * 16 - 1: the live entries of a group are distinct block rows of that range and come first, followed by -1; a group holds 4 to 8 live entries, and in every panel some group holds exactly 8.
All inputs are finite; a program needn't handle non-finite values.
Results may differ from a plain program's by a relative error of at most 0.0033.
Values may be sent and summed in bfloat16 or wider, within the bound.
No kernel may reach another device: no remote copies, remote signals or barrier semaphores. Data moves between devices by JAX's collectives and lax.ppermute only.
A program may use at most 64 MiB of HBM per device.

v0:
```python
import functools

import jax
import jax.numpy as jnp
from jax import lax
from jax.experimental import pallas as pl
from jax.experimental.pallas import tpu as pltpu
from jax.sharding import PartitionSpec as P


def _update_kernel(u_starts, n_l, rows, table_ref, trailing_ref, *refs):
    n_u = len(u_starts) - 1
    u_hbm = refs[:n_u]
    l_hbm = refs[n_u:n_u + n_l]
    out_ref = refs[n_u + n_l]
    u_scr, l_scr, lrow, sems = refs[n_u + n_l + 1:]
    side = l_scr.shape[-1]
    held = (l_scr.shape[0] - 1) // n_l
    step = pl.program_id(0)

    @pl.when(step == 0)
    def _():
        copies = [
            pltpu.make_async_copy(
                u_hbm[j],
                u_scr.at[pl.ds(u_starts[j], u_starts[j + 1] - u_starts[j])],
                sems.at[j],
            )
            for j in range(n_u)
        ] + [
            pltpu.make_async_copy(l_hbm[j], l_scr.at[pl.ds(j * held, held)], sems.at[n_u + j])
            for j in range(n_l)
        ]
        for c in copies:
            c.start()
        l_scr[n_l * held] = jnp.zeros((side, side), l_scr.dtype)
        for c in copies:
            c.wait()

    groups = rows // side
    panels = lrow.shape[1] // side
    for r in range(groups):
        for p in range(panels):
            idx = table_ref[p, step * groups + r]
            lrow[r * side:(r + 1) * side, p * side:(p + 1) * side] = l_scr[idx]
    tile = 256
    for n in range(out_ref.shape[1] // tile):
        cols = slice(n * tile, (n + 1) * tile)
        acc = jnp.dot(lrow[...], u_scr[:, cols], preferred_element_type=jnp.float32)
        out_ref[:, cols] = (trailing_ref[:, cols].astype(jnp.float32) - acc).astype(out_ref.dtype)


def fused_update(table, trailing, u_pieces, l_pieces):
    rows = 1024
    side = l_pieces[0].shape[-1]
    held = l_pieces[0].shape[0]
    n_u, n_l = len(u_pieces), len(l_pieces)
    m, n = trailing.shape
    u_starts = [0]
    for piece in u_pieces:
        u_starts.append(u_starts[-1] + piece.shape[0])
    k = u_starts[-1]
    kernel = functools.partial(_update_kernel, tuple(u_starts), n_l, rows)
    any_spec = pl.BlockSpec(memory_space=pl.ANY)
    grid_spec = pltpu.PrefetchScalarGridSpec(
        num_scalar_prefetch=1,
        grid=(m // rows,),
        in_specs=[pl.BlockSpec((rows, n), lambda g, t: (g, 0))] + [any_spec] * (n_u + n_l),
        out_specs=pl.BlockSpec((rows, n), lambda g, t: (g, 0)),
        scratch_shapes=[
            pltpu.VMEM((k, n), u_pieces[0].dtype),
            pltpu.VMEM((n_l * held + 1, side, side), l_pieces[0].dtype),
            pltpu.VMEM((rows, k), l_pieces[0].dtype),
            pltpu.SemaphoreType.DMA((n_u + n_l,)),
        ],
    )
    return pl.pallas_call(
        kernel,
        grid_spec=grid_spec,
        out_shape=jax.ShapeDtypeStruct((m, n), trailing.dtype),
        compiler_params=pltpu.CompilerParams(
            dimension_semantics=("arbitrary",), vmem_limit_bytes=48 * 1024 * 1024
        ),
        cost_estimate=pl.CostEstimate(
            flops=2 * m * k * n, transcendentals=0, bytes_accessed=2 * (2 * m * n + k * n + n_l * held * side * side)
        ),
    )(table, trailing, *u_pieces, *l_pieces)


def per_device(trailing, lower_slot_blocks, l_rows, d_inv, u_panel, pivot):
    side = d_inv.shape[-1]
    row_blocks = trailing.shape[0] // side
    col_count = trailing.shape[1]
    panels, slot_count = l_rows.shape
    n_rows = lax.axis_size("prow")
    u_own = pivot.shape[0]

    fragments = lower_slot_blocks.reshape(-1, slot_count, side, side)
    scaled = jnp.einsum(
        "ksab,kbc->ksac", fragments, d_inv, preferred_element_type=jnp.float32
    ).astype(jnp.bfloat16)
    upper_rows = u_panel.reshape(-1, side, col_count)
    lanes = jnp.arange(side, dtype=jnp.int32)
    permuting = (pivot[:, :, None] == lanes[None, None, :]).astype(jnp.bfloat16)
    pivoted = jnp.einsum(
        "kpq,kqn->kpn", permuting, upper_rows, preferred_element_type=jnp.float32
    ).astype(jnp.bfloat16).reshape(-1, col_count)
    me = lax.axis_index("prow")
    x_step = 2

    def shifted(piece, by):
        return lax.ppermute(piece, "prow", [(i, (i + by) % n_rows) for i in range(n_rows)])

    crossed_u = lax.ppermute(pivoted, "prow", [(i, i ^ 1) for i in range(n_rows)])
    pieces = []
    panel_list = []
    for base, flip in ((pivoted, 0), (crossed_u, 1)):
        right = shifted(base, x_step)
        left = shifted(base, -x_step)
        far = shifted(right, x_step) if flip == 0 else shifted(left, -x_step)
        pieces += [base, right, left, far]
        sources = [
            me ^ flip,
            ((me - x_step) % n_rows) ^ flip,
            ((me + x_step) % n_rows) ^ flip,
            ((me + 2 * x_step) % n_rows) ^ flip,
        ]
        for q in sources:
            panel_list += [u_own * q + j for j in range(u_own)]
    order = jnp.stack(panel_list)

    n_cols = lax.axis_size("pcol")
    col = lax.axis_index("pcol")
    z_step = 4
    crossed = lax.ppermute(scaled, "pcol", [(i, i ^ 2) for i in range(n_cols)])
    held = [scaled, crossed]
    for base in (scaled, crossed):
        for hop in range(1, n_cols // z_step):
            held.append(
                lax.ppermute(
                    base, "pcol", [(i, (i + z_step * hop) % n_cols) for i in range(n_cols)]
                )
            )
    swapped = [lax.ppermute(piece, "pcol", [(i, i ^ 1) for i in range(n_cols)]) for piece in held]

    def lower_sources(c):
        hops = [(c - z_step * hop) % n_cols for hop in range(1, n_cols // z_step)]
        return [c, c ^ 2] + hops + [h ^ 2 for h in hops]

    lower_order = jnp.stack(lower_sources(col) + lower_sources(col ^ 1))
    panel_ids = jnp.arange(panels, dtype=jnp.int32)
    lower_pos = jnp.sum(
        jnp.where(lower_order[None, :] == panel_ids[:, None], panel_ids[None, :], 0), axis=1
    )

    local_ids = jnp.where(l_rows >= 0, l_rows - me * row_blocks, -1)
    levels = jnp.arange(row_blocks, dtype=jnp.int32)
    hit = local_ids[:, None, :] == levels[None, :, None]
    present = jnp.any(hit, axis=-1)
    slot_of = jnp.sum(jnp.where(hit, jnp.arange(slot_count, dtype=jnp.int32), 0), axis=-1)
    table = jnp.where(
        present[order], lower_pos[order][:, None] * slot_count + slot_of[order], panels * slot_count
    )
    l_pieces = [piece.reshape(-1, side, side) for piece in held + swapped]
    return fused_update(table, trailing, pieces, l_pieces)


def solution(mesh):
    placed = (
        P("prow", "pcol"),
        P("pcol", "prow", None),
        P(None, "prow"),
        P("pcol", None, None),
        P("prow", "pcol"),
        P("prow", None),
    )

    return jax.shard_map(
        per_device, mesh=mesh, in_specs=placed, out_specs=P("prow", "pcol"), check_vma=False
    )
```

profile of v0, /device:TPU:0, one launch (start us, length us, event | category | flops | bytes accessed | tf_op | source)
XLA Modules:
  0.0 95.0 jit_solution(2749722383454572262)
XLA Ops:
  0.0 1.2 %convolution_convert_fusion.1.refs_8_ = bf16[8,128,128]{2,1,0:T(8,128)(2,1)S(1)} fusion(bf16[8,128,128]{2,1,0:T(8,128)(2,1)} %bitcast.77, bf16[1,128,128]{2,1,0:T(8,128)(2,1)} %param.9), kind=kOutput, calls=%fused_computation.4 | convolution fusion | flops 33685504 | bytes 557056 | tf_op jit(solution)/shard_map/ksab,kbc->ksac/dot_general | solution.py:99
  1.2 0.1 collective-permute-start.14
  1.3 4.2 %collective-permute-start.10 = (bf16[1,8,128,128]{3,2,1,0:T(8,128)(2,1)S(1)}, bf16[1,8,128,128]{3,2,1,0:T(8,128)(2,1)S(1)}, u32[]{:S(2)}, u32[]{:S(2)}) collective-permute-start(bf16[1,8,128,128]{3,2,1,0:T(8,128)(2,1)S(1)} %bitcast.65), channel_id=1, source_target_pairs={{0,12},{1,13},{2,14},{3,15},{4,0},{5,1},{6,2},{7,3},{8,4},{9,5},{1... | collective-permute-start | bytes 786440 | tf_op jit(solution)/shard_map/ppermute | solution.py:140
  5.5 0.0 collective-permute-start.9
  5.5 1.3 %collective-permute-start.8 = (bf16[1,8,128,128]{3,2,1,0:T(8,128)(2,1)S(1)}, bf16[1,8,128,128]{3,2,1,0:T(8,128)(2,1)S(1)}, u32[]{:S(2)}, u32[]{:S(2)}) collective-permute-start(bf16[1,8,128,128]{3,2,1,0:T(8,128)(2,1)S(1)} %bitcast.67), channel_id=1, source_target_pairs={{0,4},{1,5},{2,6},{3,7},{4,8},{5,9},{6,10},{7,11},{8,12},{9,13},{1... | collective-permute-start | bytes 786440 | tf_op jit(solution)/shard_map/ppermute | solution.py:140
  6.8 1.0 %convolution_convert_fusion = bf16[2,128,1024]{2,1,0:T(8,128)(2,1)S(1)} fusion(bf16[2,128,1024]{2,1,0:T(8,128)(2,1)S(1)} %bitcast.59, s32[2,128]{1,0:T(2,128)} %param.11), kind=kOutput, calls=%fused_computation.3 | convolution fusion | flops 67403776 | bytes 1049600 | tf_op jit(solution)/shard_map/kpq,kqn->kpn/dot_general | solution.py:105
  7.8 1.7 %collective-permute-start.3 = (bf16[256,1024]{1,0:T(8,128)(2,1)S(1)}, bf16[256,1024]{1,0:T(8,128)(2,1)}, u32[]{:S(2)}, u32[]{:S(2)}) collective-permute-start(bf16[256,1024]{1,0:T(8,128)(2,1)S(1)} %bitcast.60), channel_id=1, source_target_pairs={{0,16},{16,0},{32,48},{48,32},{64,80},{80,64},{96,112},{112,96},{1... | collective-permute-start | bytes 1572872 | tf_op jit(solution)/shard_map/ppermute | solution.py:114
  9.5 0.0 collective-permute-done.14
  9.5 2.9 %collective-permute-start.7 = (bf16[1,8,128,128]{3,2,1,0:T(8,128)(2,1)S(1)}, bf16[1,8,128,128]{3,2,1,0:T(8,128)(2,1)}, u32[]{:S(2)}, u32[]{:S(2)}) collective-permute-start(bf16[1,8,128,128]{3,2,1,0:T(8,128)(2,1)S(1)} %bitcast.68), channel_id=1, source_target_pairs={{0,2},{1,3},{2,0},{3,1},{4,6},{5,7},{6,4},{7,5},{8,10},{9,11},{10,... | collective-permute-start | bytes 786440 | tf_op jit(solution)/shard_map/ppermute | solution.py:135
  12.4 4.9 %collective-permute-done.10 = bf16[1,8,128,128]{3,2,1,0:T(8,128)(2,1)S(1)} collective-permute-done((bf16[1,8,128,128]{3,2,1,0:T(8,128)(2,1)S(1)}, bf16[1,8,128,128]{3,2,1,0:T(8,128)(2,1)S(1)}, u32[]{:S(2)}, u32[]{:S(2)}) %collective-permute-start.10) | collective-permute-done | bytes 262176 | tf_op jit(solution)/shard_map/ppermute | solution.py:140
  17.3 0.0 collective-permute-start.18
  17.3 0.0 collective-permute-done.9
  17.3 0.5 collective-permute-start.17
  17.8 2.9 %collective-permute-done.8 = bf16[1,8,128,128]{3,2,1,0:T(8,128)(2,1)S(1)} collective-permute-done((bf16[1,8,128,128]{3,2,1,0:T(8,128)(2,1)S(1)}, bf16[1,8,128,128]{3,2,1,0:T(8,128)(2,1)S(1)}, u32[]{:S(2)}, u32[]{:S(2)}) %collective-permute-start.8) | collective-permute-done | bytes 262176 | tf_op jit(solution)/shard_map/ppermute | solution.py:140
  20.7 0.0 collective-permute-start.16
  20.7 8.8 %collective-permute-done.7 = bf16[1,8,128,128]{3,2,1,0:T(8,128)(2,1)} collective-permute-done((bf16[1,8,128,128]{3,2,1,0:T(8,128)(2,1)S(1)}, bf16[1,8,128,128]{3,2,1,0:T(8,128)(2,1)}, u32[]{:S(2)}, u32[]{:S(2)}) %collective-permute-start.7) | collective-permute-done | bytes 262176 | tf_op jit(solution)/shard_map/ppermute | solution.py:135
  29.5 0.7 copy-done.1
  30.2 2.3 %collective-permute-start.13 = (bf16[1,8,128,128]{3,2,1,0:T(8,128)(2,1)}, bf16[1,8,128,128]{3,2,1,0:T(8,128)(2,1)}, u32[]{:S(2)}, u32[]{:S(2)}) collective-permute-start(bf16[1,8,128,128]{3,2,1,0:T(8,128)(2,1)} %collective-permute-done.7), channel_id=1, source_target_pairs={{0,12},{1,13},{2,14},{3,15},{4,0},{5,1},{6,2},{7,3},{8,4},{9,5},{1... | collective-permute-start | bytes 786440 | tf_op jit(solution)/shard_map/ppermute | solution.py:140
  32.5 0.7 subtract_select_fusion
  33.1 0.1 stack.118
  33.3 0.0 collective-permute-done.17
  33.3 0.7 copy-done.3
  34.0 1.5 %collective-permute-start = (bf16[256,1024]{1,0:T(8,128)(2,1)S(1)}, bf16[256,1024]{1,0:T(8,128)(2,1)S(1)}, u32[]{:S(2)}, u32[]{:S(2)}) collective-permute-start(bf16[256,1024]{1,0:T(8,128)(2,1)S(1)} %bitcast.61), channel_id=1, source_target_pairs={{0,32},{16,48},{32,64},{48,80},{64,96},{80,112},{96,0},{112,16},{1... | collective-permute-start | bytes 1572872 | tf_op jit(solution)/shard_map/ppermute | solution.py:112
  35.5 0.0 collective-permute-done.16
  35.5 0.7 copy-done.5
  36.2 2.0 %collective-permute-start.12 = (bf16[1,8,128,128]{3,2,1,0:T(8,128)(2,1)}, bf16[1,8,128,128]{3,2,1,0:T(8,128)(2,1)}, u32[]{:S(2)}, u32[]{:S(2)}) collective-permute-start(bf16[1,8,128,128]{3,2,1,0:T(8,128)(2,1)} %collective-permute-done.7), channel_id=1, source_target_pairs={{0,8},{1,9},{2,10},{3,11},{4,12},{5,13},{6,14},{7,15},{8,0},{9,1},... | collective-permute-start | bytes 786440 | tf_op jit(solution)/shard_map/ppermute | solution.py:140
  38.2 0.0 collective-permute-done.3.refs_4_
  38.2 1.8 %collective-permute-start.5 = (bf16[256,1024]{1,0:T(8,128)(2,1)}, bf16[256,1024]{1,0:T(8,128)(2,1)}, u32[]{:S(2)}, u32[]{:S(2)}) collective-permute-start(bf16[256,1024]{1,0:T(8,128)(2,1)} %collective-permute-done.3.refs_4_), channel_id=1, source_target_pairs={{0,96},{16,112},{32,0},{48,16},{64,32},{80,48},{96,64},{112,80},{1... | collective-permute-start | bytes 1572872 | tf_op jit(solution)/shard_map/ppermute | solution.py:112
  40.0 0.1 stack.135
  40.1 0.0 collective-permute-done.15
  40.1 0.0 copy-start.7
  40.1 0.7 copy-done.7
  40.8 1.5 %collective-permute-start.1 = (bf16[256,1024]{1,0:T(8,128)(2,1)S(1)}, bf16[256,1024]{1,0:T(8,128)(2,1)S(1)}, u32[]{:S(2)}, u32[]{:S(2)}) collective-permute-start(bf16[256,1024]{1,0:T(8,128)(2,1)S(1)} %bitcast.62), channel_id=1, source_target_pairs={{0,96},{16,112},{32,0},{48,16},{64,32},{80,48},{96,64},{112,80},{1... | collective-permute-start | bytes 1572872 | tf_op jit(solution)/shard_map/ppermute | solution.py:112
  42.3 2.3 %collective-permute-done.13 = bf16[1,8,128,128]{3,2,1,0:T(8,128)(2,1)} collective-permute-done((bf16[1,8,128,128]{3,2,1,0:T(8,128)(2,1)}, bf16[1,8,128,128]{3,2,1,0:T(8,128)(2,1)}, u32[]{:S(2)}, u32[]{:S(2)}) %collective-permute-start.13) | collective-permute-done | bytes 262176 | tf_op jit(solution)/shard_map/ppermute | solution.py:140
  44.7 2.4 %collective-permute-start.11 = (bf16[1,8,128,128]{3,2,1,0:T(8,128)(2,1)}, bf16[1,8,128,128]{3,2,1,0:T(8,128)(2,1)}, u32[]{:S(2)}, u32[]{:S(2)}) collective-permute-start(bf16[1,8,128,128]{3,2,1,0:T(8,128)(2,1)} %collective-permute-done.7), channel_id=1, source_target_pairs={{0,4},{1,5},{2,6},{3,7},{4,8},{5,9},{6,10},{7,11},{8,12},{9,13},{1... | collective-permute-start | bytes 786440 | tf_op jit(solution)/shard_map/ppermute | solution.py:140
  47.1 0.1 select_reduce_fusion.1
  47.2 0.1 copy.9
  47.3 0.1 fusion.1
  47.4 0.0 collective-permute-done.12
  47.4 0.1 collective-permute-start.21
  47.5 0.7 gather_fusion.1
  48.2 4.8 %collective-permute-done.11 = bf16[1,8,128,128]{3,2,1,0:T(8,128)(2,1)} collective-permute-done((bf16[1,8,128,128]{3,2,1,0:T(8,128)(2,1)}, bf16[1,8,128,128]{3,2,1,0:T(8,128)(2,1)}, u32[]{:S(2)}, u32[]{:S(2)}) %collective-permute-start.11) | collective-permute-done | bytes 262176 | tf_op jit(solution)/shard_map/ppermute | solution.py:140
  53.0 1.5 %collective-permute-start.4 = (bf16[256,1024]{1,0:T(8,128)(2,1)}, bf16[256,1024]{1,0:T(8,128)(2,1)}, u32[]{:S(2)}, u32[]{:S(2)}) collective-permute-start(bf16[256,1024]{1,0:T(8,128)(2,1)} %collective-permute-done.3.refs_4_), channel_id=1, source_target_pairs={{0,32},{16,48},{32,64},{48,80},{64,96},{80,112},{96,0},{112,16},{1... | collective-permute-start | bytes 1572872 | tf_op jit(solution)/shard_map/ppermute | solution.py:112
  54.5 1.5 %collective-permute-start.2 = (bf16[256,1024]{1,0:T(8,128)(2,1)S(1)}, bf16[256,1024]{1,0:T(8,128)(2,1)}, u32[]{:S(2)}, u32[]{:S(2)}) collective-permute-start(bf16[256,1024]{1,0:T(8,128)(2,1)S(1)} %collective-permute-done.refs_1_), channel_id=1, source_target_pairs={{0,32},{16,48},{32,64},{48,80},{64,96},{80,112},{96,0},{112,16},{1... | collective-permute-start | bytes 1572872 | tf_op jit(solution)/shard_map/ppermute | solution.py:112
  56.0 0.0 collective-permute-done.5.refs_6_
  56.0 1.7 %collective-permute-start.6 = (bf16[256,1024]{1,0:T(8,128)(2,1)}, bf16[256,1024]{1,0:T(8,128)(2,1)}, u32[]{:S(2)}, u32[]{:S(2)}) collective-permute-start(bf16[256,1024]{1,0:T(8,128)(2,1)} %collective-permute-done.5.refs_6_), channel_id=1, source_target_pairs={{0,96},{16,112},{32,0},{48,16},{64,32},{80,48},{96,64},{112,80},{1... | collective-permute-start | bytes 1572872 | tf_op jit(solution)/shard_map/ppermute | solution.py:112
  57.7 6.7 %collective-permute-done.1.refs_2_ = bf16[256,1024]{1,0:T(8,128)(2,1)S(1)} collective-permute-done((bf16[256,1024]{1,0:T(8,128)(2,1)S(1)}, bf16[256,1024]{1,0:T(8,128)(2,1)S(1)}, u32[]{:S(2)}, u32[]{:S(2)}) %collective-permute-start.1) | collective-permute-done | bytes 524320 | tf_op jit(solution)/shard_map/ppermute | solution.py:112
  64.4 0.0 collective-permute-start.20
  64.4 0.0 collective-permute-done.21
  64.4 0.5 collective-permute-start.19
  65.0 0.1 select_reduce_fusion
  65.1 0.6 gather_fusion.2
  65.6 0.6 gather_fusion
  66.2 0.1 add_select_fusion.table_ref
  66.3 0.0 collective-permute-done.20
  66.3 0.4 collective-permute-done.19
  66.7 2.6 %collective-permute-done.4.refs_5_ = bf16[256,1024]{1,0:T(8,128)(2,1)} collective-permute-done((bf16[256,1024]{1,0:T(8,128)(2,1)}, bf16[256,1024]{1,0:T(8,128)(2,1)}, u32[]{:S(2)}, u32[]{:S(2)}) %collective-permute-start.4) | collective-permute-done | bytes 524320 | tf_op jit(solution)/shard_map/ppermute | solution.py:112
  69.3 6.5 %collective-permute-done.2.refs_3_ = bf16[256,1024]{1,0:T(8,128)(2,1)} collective-permute-done((bf16[256,1024]{1,0:T(8,128)(2,1)S(1)}, bf16[256,1024]{1,0:T(8,128)(2,1)}, u32[]{:S(2)}, u32[]{:S(2)}) %collective-permute-start.2) | collective-permute-done | bytes 524320 | tf_op jit(solution)/shard_map/ppermute | solution.py:112
  75.8 0.0 collective-permute-done.6.refs_7_
  75.8 0.9 copy-done.2
  76.7 0.9 copy-done.4
  77.7 0.9 copy-done.6
  78.6 0.9 copy-done.8
  79.6 15.4 %shard_map.64 = bf16[2048,1024]{1,0:T(8,128)(2,1)} custom-call(s32[16,16]{1,0:T(8,128)S(1)} %add_select_fusion.table_ref, bf16[2048,1024]{1,0:T(8,128)(2,1)} %trailing_ref.1, bf16[256,1024]{1,0:T(8,128)(2,1)S(1)} %bitcast.63, bf16[256,1024]{1,0:T(8,128)(2,1)S(1)} %collective-permute-done.refs_1_, bf16[256,1024]{1,0:T(8,128)(2,1)S(1)} %collective-permute-done.1.refs_2_, ...), custom_call_target="tpu_custom_call" | custom-call | flops 8589934592 | bytes 16777216 | tf_op jit(solution)/shard_map/pallas_call | solution.py:77
  (15 shorter events, 0.0 us)
Async XLA Ops:
  0.0 6.8 %copy-start = (bf16[256,1024]{1,0:T(8,128)(2,1)S(1)}, bf16[256,1024]{1,0:T(8,128)(2,1)}, u32[]{:S(2)}) copy-start(bf16[256,1024]{1,0:T(8,128)(2,1)} %param.10) | copy-start | bytes 1572868
  1.2 8.3 %collective-permute-start.14 = (bf16[1,8,128,128]{3,2,1,0:T(8,128)(2,1)S(1)}, bf16[1,8,128,128]{3,2,1,0:T(8,128)(2,1)S(1)}, u32[]{:S(2)}, u32[]{:S(2)}) collective-permute-start(bf16[1,8,128,128]{3,2,1,0:T(8,128)(2,1)S(1)} %bitcast.64), channel_id=1, source_target_pairs={{0,1},{1,0},{2,3},{3,2},{4,5},{5,4},{6,7},{7,6},{8,9},{9,8},{10,11... | collective-permute-start | bytes 786440 | tf_op jit(solution)/shard_map/ppermute | solution.py:144
  1.3 16.0 %collective-permute-start.10 = (bf16[1,8,128,128]{3,2,1,0:T(8,128)(2,1)S(1)}, bf16[1,8,128,128]{3,2,1,0:T(8,128)(2,1)S(1)}, u32[]{:S(2)}, u32[]{:S(2)}) collective-permute-start(bf16[1,8,128,128]{3,2,1,0:T(8,128)(2,1)S(1)} %bitcast.65), channel_id=1, source_target_pairs={{0,12},{1,13},{2,14},{3,15},{4,0},{5,1},{6,2},{7,3},{8,4},{9,5},{1... | collective-permute-start | bytes 786440 | tf_op jit(solution)/shard_map/ppermute | solution.py:140
  5.5 11.8 %collective-permute-start.9 = (bf16[1,8,128,128]{3,2,1,0:T(8,128)(2,1)S(1)}, bf16[1,8,128,128]{3,2,1,0:T(8,128)(2,1)S(1)}, u32[]{:S(2)}, u32[]{:S(2)}) collective-permute-start(bf16[1,8,128,128]{3,2,1,0:T(8,128)(2,1)S(1)} %bitcast.66), channel_id=1, source_target_pairs={{0,8},{1,9},{2,10},{3,11},{4,12},{5,13},{6,14},{7,15},{8,0},{9,1},... | collective-permute-start | bytes 786440 | tf_op jit(solution)/shard_map/ppermute | solution.py:140
  5.5 15.2 %collective-permute-start.8 = (bf16[1,8,128,128]{3,2,1,0:T(8,128)(2,1)S(1)}, bf16[1,8,128,128]{3,2,1,0:T(8,128)(2,1)S(1)}, u32[]{:S(2)}, u32[]{:S(2)}) collective-permute-start(bf16[1,8,128,128]{3,2,1,0:T(8,128)(2,1)S(1)} %bitcast.67), channel_id=1, source_target_pairs={{0,4},{1,5},{2,6},{3,7},{4,8},{5,9},{6,10},{7,11},{8,12},{9,13},{1... | collective-permute-start | bytes 786440 | tf_op jit(solution)/shard_map/ppermute | solution.py:140
  7.8 30.4 %collective-permute-start.3 = (bf16[256,1024]{1,0:T(8,128)(2,1)S(1)}, bf16[256,1024]{1,0:T(8,128)(2,1)}, u32[]{:S(2)}, u32[]{:S(2)}) collective-permute-start(bf16[256,1024]{1,0:T(8,128)(2,1)S(1)} %bitcast.60), channel_id=1, source_target_pairs={{0,16},{16,0},{32,48},{48,32},{64,80},{80,64},{96,112},{112,96},{1... | collective-permute-start | bytes 1572872 | tf_op jit(solution)/shard_map/ppermute | solution.py:114
  9.5 20.0 %collective-permute-start.7 = (bf16[1,8,128,128]{3,2,1,0:T(8,128)(2,1)S(1)}, bf16[1,8,128,128]{3,2,1,0:T(8,128)(2,1)}, u32[]{:S(2)}, u32[]{:S(2)}) collective-permute-start(bf16[1,8,128,128]{3,2,1,0:T(8,128)(2,1)S(1)} %bitcast.68), channel_id=1, source_target_pairs={{0,2},{1,3},{2,0},{3,1},{4,6},{5,7},{6,4},{7,5},{8,10},{9,11},{10,... | collective-permute-start | bytes 786440 | tf_op jit(solution)/shard_map/ppermute | solution.py:135
  17.3 12.2 %collective-permute-start.18 = (bf16[1,8,128,128]{3,2,1,0:T(8,128)(2,1)S(1)}, bf16[1,8,128,128]{3,2,1,0:T(8,128)(2,1)S(1)}, u32[]{:S(2)}, u32[]{:S(2)}) collective-permute-start(bf16[1,8,128,128]{3,2,1,0:T(8,128)(2,1)S(1)} %collective-permute-done.10), channel_id=1, source_target_pairs={{0,1},{1,0},{2,3},{3,2},{4,5},{5,4},{6,7},{7,6},{8,9},{9,8},{10,11... | collective-permute-start | bytes 786440 | tf_op jit(solution)/shard_map/ppermute | solution.py:144
  17.3 15.9 %collective-permute-start.17 = (bf16[1,8,128,128]{3,2,1,0:T(8,128)(2,1)S(1)}, bf16[1,8,128,128]{3,2,1,0:T(8,128)(2,1)S(1)}, u32[]{:S(2)}, u32[]{:S(2)}) collective-permute-start(bf16[1,8,128,128]{3,2,1,0:T(8,128)(2,1)S(1)} %collective-permute-done.9), channel_id=1, source_target_pairs={{0,1},{1,0},{2,3},{3,2},{4,5},{5,4},{6,7},{7,6},{8,9},{9,8},{10,11... | collective-permute-start | bytes 786440 | tf_op jit(solution)/shard_map/ppermute | solution.py:144
  20.7 14.7 %collective-permute-start.16 = (bf16[1,8,128,128]{3,2,1,0:T(8,128)(2,1)S(1)}, bf16[1,8,128,128]{3,2,1,0:T(8,128)(2,1)S(1)}, u32[]{:S(2)}, u32[]{:S(2)}) collective-permute-start(bf16[1,8,128,128]{3,2,1,0:T(8,128)(2,1)S(1)} %collective-permute-done.8), channel_id=1, source_target_pairs={{0,1},{1,0},{2,3},{3,2},{4,5},{5,4},{6,7},{7,6},{8,9},{9,8},{10,11... | collective-permute-start | bytes 786440 | tf_op jit(solution)/shard_map/ppermute | solution.py:144
  29.5 10.6 %collective-permute-start.15 = (bf16[1,8,128,128]{3,2,1,0:T(8,128)(2,1)}, bf16[1,8,128,128]{3,2,1,0:T(8,128)(2,1)S(1)}, u32[]{:S(2)}, u32[]{:S(2)}) collective-permute-start(bf16[1,8,128,128]{3,2,1,0:T(8,128)(2,1)} %collective-permute-done.7), channel_id=1, source_target_pairs={{0,1},{1,0},{2,3},{3,2},{4,5},{5,4},{6,7},{7,6},{8,9},{9,8},{10,11... | collective-permute-start | bytes 786440 | tf_op jit(solution)/shard_map/ppermute | solution.py:144
  29.5 0.7 copy-start.1
  30.2 14.5 %collective-permute-start.13 = (bf16[1,8,128,128]{3,2,1,0:T(8,128)(2,1)}, bf16[1,8,128,128]{3,2,1,0:T(8,128)(2,1)}, u32[]{:S(2)}, u32[]{:S(2)}) collective-permute-start(bf16[1,8,128,128]{3,2,1,0:T(8,128)(2,1)} %collective-permute-done.7), channel_id=1, source_target_pairs={{0,12},{1,13},{2,14},{3,15},{4,0},{5,1},{6,2},{7,3},{8,4},{9,5},{1... | collective-permute-start | bytes 786440 | tf_op jit(solution)/shard_map/ppermute | solution.py:140
  33.3 0.7 copy-start.3
  34.0 20.5 %collective-permute-start = (bf16[256,1024]{1,0:T(8,128)(2,1)S(1)}, bf16[256,1024]{1,0:T(8,128)(2,1)S(1)}, u32[]{:S(2)}, u32[]{:S(2)}) collective-permute-start(bf16[256,1024]{1,0:T(8,128)(2,1)S(1)} %bitcast.61), channel_id=1, source_target_pairs={{0,32},{16,48},{32,64},{48,80},{64,96},{80,112},{96,0},{112,16},{1... | collective-permute-start | bytes 1572872 | tf_op jit(solution)/shard_map/ppermute | solution.py:112
  35.5 0.7 copy-start.5
  36.2 11.2 %collective-permute-start.12 = (bf16[1,8,128,128]{3,2,1,0:T(8,128)(2,1)}, bf16[1,8,128,128]{3,2,1,0:T(8,128)(2,1)}, u32[]{:S(2)}, u32[]{:S(2)}) collective-permute-start(bf16[1,8,128,128]{3,2,1,0:T(8,128)(2,1)} %collective-permute-done.7), channel_id=1, source_target_pairs={{0,8},{1,9},{2,10},{3,11},{4,12},{5,13},{6,14},{7,15},{8,0},{9,1},... | collective-permute-start | bytes 786440 | tf_op jit(solution)/shard_map/ppermute | solution.py:140
  38.2 17.8 %collective-permute-start.5 = (bf16[256,1024]{1,0:T(8,128)(2,1)}, bf16[256,1024]{1,0:T(8,128)(2,1)}, u32[]{:S(2)}, u32[]{:S(2)}) collective-permute-start(bf16[256,1024]{1,0:T(8,128)(2,1)} %collective-permute-done.3.refs_4_), channel_id=1, source_target_pairs={{0,96},{16,112},{32,0},{48,16},{64,32},{80,48},{96,64},{112,80},{1... | collective-permute-start | bytes 1572872 | tf_op jit(solution)/shard_map/ppermute | solution.py:112
  40.1 0.7 copy-start.7
  40.8 23.7 %collective-permute-start.1 = (bf16[256,1024]{1,0:T(8,128)(2,1)S(1)}, bf16[256,1024]{1,0:T(8,128)(2,1)S(1)}, u32[]{:S(2)}, u32[]{:S(2)}) collective-permute-start(bf16[256,1024]{1,0:T(8,128)(2,1)S(1)} %bitcast.62), channel_id=1, source_target_pairs={{0,96},{16,112},{32,0},{48,16},{64,32},{80,48},{96,64},{112,80},{1... | collective-permute-start | bytes 1572872 | tf_op jit(solution)/shard_map/ppermute | solution.py:112
  44.7 8.3 %collective-permute-start.11 = (bf16[1,8,128,128]{3,2,1,0:T(8,128)(2,1)}, bf16[1,8,128,128]{3,2,1,0:T(8,128)(2,1)}, u32[]{:S(2)}, u32[]{:S(2)}) collective-permute-start(bf16[1,8,128,128]{3,2,1,0:T(8,128)(2,1)} %collective-permute-done.7), channel_id=1, source_target_pairs={{0,4},{1,5},{2,6},{3,7},{4,8},{5,9},{6,10},{7,11},{8,12},{9,13},{1... | collective-permute-start | bytes 786440 | tf_op jit(solution)/shard_map/ppermute | solution.py:140
  47.4 17.1 %collective-permute-start.21 = (bf16[1,8,128,128]{3,2,1,0:T(8,128)(2,1)}, bf16[1,8,128,128]{3,2,1,0:T(8,128)(2,1)}, u32[]{:S(2)}, u32[]{:S(2)}) collective-permute-start(bf16[1,8,128,128]{3,2,1,0:T(8,128)(2,1)} %collective-permute-done.13), channel_id=1, source_target_pairs={{0,1},{1,0},{2,3},{3,2},{4,5},{5,4},{6,7},{7,6},{8,9},{9,8},{10,11... | collective-permute-start | bytes 786440 | tf_op jit(solution)/shard_map/ppermute | solution.py:144
  53.0 16.3 %collective-permute-start.4 = (bf16[256,1024]{1,0:T(8,128)(2,1)}, bf16[256,1024]{1,0:T(8,128)(2,1)}, u32[]{:S(2)}, u32[]{:S(2)}) collective-permute-start(bf16[256,1024]{1,0:T(8,128)(2,1)} %collective-permute-done.3.refs_4_), channel_id=1, source_target_pairs={{0,32},{16,48},{32,64},{48,80},{64,96},{80,112},{96,0},{112,16},{1... | collective-permute-start | bytes 1572872 | tf_op jit(solution)/shard_map/ppermute | solution.py:112
  54.5 21.3 %collective-permute-start.2 = (bf16[256,1024]{1,0:T(8,128)(2,1)S(1)}, bf16[256,1024]{1,0:T(8,128)(2,1)}, u32[]{:S(2)}, u32[]{:S(2)}) collective-permute-start(bf16[256,1024]{1,0:T(8,128)(2,1)S(1)} %collective-permute-done.refs_1_), channel_id=1, source_target_pairs={{0,32},{16,48},{32,64},{48,80},{64,96},{80,112},{96,0},{112,16},{1... | collective-permute-start | bytes 1572872 | tf_op jit(solution)/shard_map/ppermute | solution.py:112
  56.0 19.8 %collective-permute-start.6 = (bf16[256,1024]{1,0:T(8,128)(2,1)}, bf16[256,1024]{1,0:T(8,128)(2,1)}, u32[]{:S(2)}, u32[]{:S(2)}) collective-permute-start(bf16[256,1024]{1,0:T(8,128)(2,1)} %collective-permute-done.5.refs_6_), channel_id=1, source_target_pairs={{0,96},{16,112},{32,0},{48,16},{64,32},{80,48},{96,64},{112,80},{1... | collective-permute-start | bytes 1572872 | tf_op jit(solution)/shard_map/ppermute | solution.py:112
  64.4 1.9 %collective-permute-start.20 = (bf16[1,8,128,128]{3,2,1,0:T(8,128)(2,1)}, bf16[1,8,128,128]{3,2,1,0:T(8,128)(2,1)}, u32[]{:S(2)}, u32[]{:S(2)}) collective-permute-start(bf16[1,8,128,128]{3,2,1,0:T(8,128)(2,1)} %collective-permute-done.12), channel_id=1, source_target_pairs={{0,1},{1,0},{2,3},{3,2},{4,5},{5,4},{6,7},{7,6},{8,9},{9,8},{10,11... | collective-permute-start | bytes 786440 | tf_op jit(solution)/shard_map/ppermute | solution.py:144
  64.4 2.2 %collective-permute-start.19 = (bf16[1,8,128,128]{3,2,1,0:T(8,128)(2,1)}, bf16[1,8,128,128]{3,2,1,0:T(8,128)(2,1)}, u32[]{:S(2)}, u32[]{:S(2)}) collective-permute-start(bf16[1,8,128,128]{3,2,1,0:T(8,128)(2,1)} %collective-permute-done.11), channel_id=1, source_target_pairs={{0,1},{1,0},{2,3},{3,2},{4,5},{5,4},{6,7},{7,6},{8,9},{9,8},{10,11... | collective-permute-start | bytes 786440 | tf_op jit(solution)/shard_map/ppermute | solution.py:144
  75.8 1.0 %copy-start.2 = (bf16[1,8,128,128]{3,2,1,0:T(8,128)(2,1)S(1)}, bf16[1,8,128,128]{3,2,1,0:T(8,128)(2,1)}, u32[]{:S(2)}) copy-start(bf16[1,8,128,128]{3,2,1,0:T(8,128)(2,1)} %copy-done.1) | copy-start | bytes 786436
  76.7 0.9 %copy-start.4 = (bf16[1,8,128,128]{3,2,1,0:T(8,128)(2,1)S(1)}, bf16[1,8,128,128]{3,2,1,0:T(8,128)(2,1)}, u32[]{:S(2)}) copy-start(bf16[1,8,128,128]{3,2,1,0:T(8,128)(2,1)} %copy-done.3) | copy-start | bytes 786436
  77.7 0.9 %copy-start.6 = (bf16[1,8,128,128]{3,2,1,0:T(8,128)(2,1)S(1)}, bf16[1,8,128,128]{3,2,1,0:T(8,128)(2,1)}, u32[]{:S(2)}) copy-start(bf16[1,8,128,128]{3,2,1,0:T(8,128)(2,1)} %copy-done.5) | copy-start | bytes 786436
  78.6 0.9 %copy-start.8 = (bf16[1,8,128,128]{3,2,1,0:T(8,128)(2,1)S(1)}, bf16[1,8,128,128]{3,2,1,0:T(8,128)(2,1)}, u32[]{:S(2)}) copy-start(bf16[1,8,128,128]{3,2,1,0:T(8,128)(2,1)} %copy-done.7) | copy-start | bytes 786436
where the time goes:
time: 95.3 us; the launch traced here: 95 us
  waiting for transfers between devices  40 us (42%)
  starting transfers between devices  27.5 us (29%)
  Pallas kernels  15.4 us (16%)
  local copies, waits for them, and re-layouts  8.65 us (9%)
  matrix products  2.24 us (2%)
  other arithmetic  1.09 us (1%)
    ppermute x6, waiting for transfers between devices, shifted(): lax.ppermute(piece, 'prow', [(i, (i + by) % n_rows) for i in range(n_rows)])  15.8 us
    pallas_call x1, Pallas kernels, fused_update(): pl.pallas_call(kernel, grid_spec=grid_spec, out_shape=jax.ShapeDtypeStruc...  15.4 us
    ppermute x6, waiting for transfers between devices, per_device(): lax.ppermute(base, 'pcol', [(i, (i + z_step * hop) % n_cols) for i in ran...  15 us
    ppermute x6, starting transfers between devices, per_device(): lax.ppermute(base, 'pcol', [(i, (i + z_step * hop) % n_cols) for i in ran...  12.2 us
    ppermute x6, starting transfers between devices, shifted(): lax.ppermute(piece, 'prow', [(i, (i + by) % n_rows) for i in range(n_rows)])  9.5 us
    ppermute x1, waiting for transfers between devices, per_device(): crossed = lax.ppermute(scaled, 'pcol', [(i, i ^ 2) for i in range(n_cols)])  8.76 us
    unnamed x18, local copies, waits for them, and re-layouts  6.58 us
    ppermute x1, starting transfers between devices, per_device(): crossed = lax.ppermute(scaled, 'pcol', [(i, i ^ 2) for i in range(n_cols)])  2.9 us
  transfers between devices with their start and end apart: 22, of which 9 were waited for; matrix products, arithmetic and copies ran while one was open for 4% of the time, Pallas kernels for 0%

commit v1 on v0

--- a/solution.py
+++ b/solution.py
@@ -50,8 +50,8 @@
         out_ref[:, cols] = (trailing_ref[:, cols].astype(jnp.float32) - acc).astype(out_ref.dtype)
 
 
-def fused_update(table, trailing, u_pieces, l_pieces):
-    rows = 1024
+def fused_update(table, trailing, u_pieces, l_pieces, out_dtype):
+    rows = 512
     side = l_pieces[0].shape[-1]
     held = l_pieces[0].shape[0]
     n_u, n_l = len(u_pieces), len(l_pieces)
@@ -77,12 +77,16 @@
     return pl.pallas_call(
         kernel,
         grid_spec=grid_spec,
-        out_shape=jax.ShapeDtypeStruct((m, n), trailing.dtype),
+        out_shape=jax.ShapeDtypeStruct((m, n), out_dtype),
         compiler_params=pltpu.CompilerParams(
             dimension_semantics=("arbitrary",), vmem_limit_bytes=48 * 1024 * 1024
         ),
         cost_estimate=pl.CostEstimate(
-            flops=2 * m * k * n, transcendentals=0, bytes_accessed=2 * (2 * m * n + k * n + n_l * held * side * side)
+            flops=2 * m * k * n,
+            transcendentals=0,
+            bytes_accessed=trailing.dtype.itemsize * m * n
+            + jnp.dtype(out_dtype).itemsize * m * n
+            + 2 * (k * n + n_l * held * side * side),
         ),
     )(table, trailing, *u_pieces, *l_pieces)
 
@@ -112,21 +116,24 @@
         return lax.ppermute(piece, "prow", [(i, (i + by) % n_rows) for i in range(n_rows)])
 
     crossed_u = lax.ppermute(pivoted, "prow", [(i, i ^ 1) for i in range(n_rows)])
-    pieces = []
-    panel_list = []
+    pieces, panel_list, late, late_panels = [], [], [], []
     for base, flip in ((pivoted, 0), (crossed_u, 1)):
         right = shifted(base, x_step)
         left = shifted(base, -x_step)
         far = shifted(right, x_step) if flip == 0 else shifted(left, -x_step)
-        pieces += [base, right, left, far]
+        pieces += [base, right, left]
+        late.append(far)
         sources = [
             me ^ flip,
             ((me - x_step) % n_rows) ^ flip,
             ((me + x_step) % n_rows) ^ flip,
-            ((me + 2 * x_step) % n_rows) ^ flip,
         ]
         for q in sources:
             panel_list += [u_own * q + j for j in range(u_own)]
+        far_source = ((me + 2 * x_step) % n_rows) ^ flip
+        late_panels += [u_own * far_source + j for j in range(u_own)]
+    early_count = len(panel_list)
+    panel_list += late_panels
     order = jnp.stack(panel_list)
 
     n_cols = lax.axis_size("pcol")
@@ -162,7 +169,8 @@
         present[order], lower_pos[order][:, None] * slot_count + slot_of[order], panels * slot_count
     )
     l_pieces = [piece.reshape(-1, side, side) for piece in held + swapped]
-    return fused_update(table, trailing, pieces, l_pieces)
+    partial = fused_update(table[:early_count], trailing, pieces, l_pieces, jnp.float32)
+    return fused_update(table[early_count:], partial, late, l_pieces, trailing.dtype)
 
 
 def solution(mesh):

time: 95.3 us -> 79.1 us (0.83)
  waiting for transfers between devices: 40 us -> 25.5 us
  Pallas kernels: 15.4 us -> 22.8 us
  local copies, waits for them, and re-layouts: 8.65 us -> 2.08 us
  starting transfers between devices: 27.5 us -> 24.9 us
    ppermute x6, waiting for transfers between devices: 15.8 us -> 4.44 us  [shifted(): lax.ppermute(piece, 'prow', [(i, (i + by) % n_rows) for i in range(n_rows)])]
    ppermute x1, waiting for transfers between devices: 8.76 us -> 0.01 us  [per_device(): crossed = lax.ppermute(scaled, 'pcol', [(i, i ^ 2) for i in range(n_cols)])]
    pallas_call x1 -> x2, Pallas kernels: 15.4 us -> 22.8 us  [fused_update(): pl.pallas_call(kernel, grid_spec=grid_spec, out_shape=jax.ShapeDtypeStruc...]
    unnamed x18 -> x2, local copies, waits for them, and re-layouts: 6.58 us -> 0.01 us
    ppermute x6, waiting for transfers between devices: 15 us -> 21.1 us  [per_device(): lax.ppermute(base, 'pcol', [(i, (i + z_step * hop) % n_cols) for i in ran...]
    ppermute x6, starting transfers between devices: 12.2 us -> 7.48 us  [per_device(): lax.ppermute(base, 'pcol', [(i, (i + z_step * hop) % n_cols) for i in ran...]
    ppermute x6, starting transfers between devices: 9.5 us -> 10.9 us  [shifted(): lax.ppermute(piece, 'prow', [(i, (i + by) % n_rows) for i in range(n_rows)])]
  transfers between devices with their start and end apart: 22 -> 22, of which waited for: 9 -> 6; matrix products, arithmetic and copies ran while one was open for 4% -> 5% of each run, Pallas kernels for 0% -> 17%
where the time goes in v1:
time: 79.1 us; the launch traced here: 78.8 us
  waiting for transfers between devices  25.5 us (32%)
  starting transfers between devices  24.9 us (31%)
  Pallas kernels  22.8 us (29%)
  matrix products  2.23 us (3%)
  local copies, waits for them, and re-layouts  2.08 us (3%)
  other arithmetic  1.09 us (1%)
    pallas_call x2, Pallas kernels, fused_update(): pl.pallas_call(kernel, grid_spec=grid_spec, out_shape=jax.ShapeDtypeStruc...  22.8 us
    ppermute x6, waiting for transfers between devices, per_device(): lax.ppermute(base, 'pcol', [(i, (i + z_step * hop) % n_cols) for i in ran...  21.1 us
    ppermute x6, starting transfers between devices, shifted(): lax.ppermute(piece, 'prow', [(i, (i + by) % n_rows) for i in range(n_rows)])  10.9 us
    ppermute x6, starting transfers between devices, per_device(): lax.ppermute(base, 'pcol', [(i, (i + z_step * hop) % n_cols) for i in ran...  7.48 us
    ppermute x6, waiting for transfers between devices, shifted(): lax.ppermute(piece, 'prow', [(i, (i + by) % n_rows) for i in range(n_rows)])  4.44 us
    ppermute x1, starting transfers between devices, per_device(): crossed = lax.ppermute(scaled, 'pcol', [(i, i ^ 2) for i in range(n_cols)])  3.19 us
    ppermute x8, starting transfers between devices, per_device(): lax.ppermute(piece, 'pcol', [(i, i ^ 1) for i in range(n_cols)])  1.7 us
    ppermute x1, starting transfers between devices, per_device(): lax.ppermute(pivoted, 'prow', [(i, i ^ 1) for i in range(n_rows)])  1.66 us
  transfers between devices with their start and end apart: 22, of which 6 were waited for; matrix products, arithmetic and copies ran while one was open for 5% of the time, Pallas kernels for 17%

profile of v1, /device:TPU:0, one launch (start us, length us, event | category | flops | bytes accessed | tf_op | source)
XLA Modules:
  0.0 78.8 jit_solution(15981176916886533439)
XLA Ops:
  0.0 0.0 copy-start
  0.0 1.2 %convolution_convert_fusion.1.refs_6_.refs_2_ = bf16[8,128,128]{2,1,0:T(8,128)(2,1)S(1)} fusion(bf16[8,128,128]{2,1,0:T(8,128)(2,1)} %bitcast.87, bf16[1,128,128]{2,1,0:T(8,128)(2,1)} %param.9), kind=kOutput, calls=%fused_computation.4 | convolution fusion | flops 33685504 | bytes 557056 | tf_op jit(solution)/shard_map/ksab,kbc->ksac/dot_general | solution.py:103
  1.2 4.2 %collective-permute-start.8 = (bf16[1,8,128,128]{3,2,1,0:T(8,128)(2,1)S(1)}, bf16[1,8,128,128]{3,2,1,0:T(8,128)(2,1)S(1)}, u32[]{:S(2)}, u32[]{:S(2)}) collective-permute-start(bf16[1,8,128,128]{3,2,1,0:T(8,128)(2,1)S(1)} %bitcast.61), channel_id=1, source_target_pairs={{0,12},{1,13},{2,14},{3,15},{4,0},{5,1},{6,2},{7,3},{8,4},{9,5},{1... | collective-permute-start | bytes 786440 | tf_op jit(solution)/shard_map/ppermute | solution.py:147
  5.4 0.0 collective-permute-start.7
  5.4 1.3 %collective-permute-start.6 = (bf16[1,8,128,128]{3,2,1,0:T(8,128)(2,1)S(1)}, bf16[1,8,128,128]{3,2,1,0:T(8,128)(2,1)S(1)}, u32[]{:S(2)}, u32[]{:S(2)}) collective-permute-start(bf16[1,8,128,128]{3,2,1,0:T(8,128)(2,1)S(1)} %bitcast.63), channel_id=1, source_target_pairs={{0,4},{1,5},{2,6},{3,7},{4,8},{5,9},{6,10},{7,11},{8,12},{9,13},{1... | collective-permute-start | bytes 786440 | tf_op jit(solution)/shard_map/ppermute | solution.py:147
  6.7 3.2 %collective-permute-start.5 = (bf16[1,8,128,128]{3,2,1,0:T(8,128)(2,1)S(1)}, bf16[1,8,128,128]{3,2,1,0:T(8,128)(2,1)S(1)}, u32[]{:S(2)}, u32[]{:S(2)}) collective-permute-start(bf16[1,8,128,128]{3,2,1,0:T(8,128)(2,1)S(1)} %bitcast.64), channel_id=1, source_target_pairs={{0,2},{1,3},{2,0},{3,1},{4,6},{5,7},{6,4},{7,5},{8,10},{9,11},{10,... | collective-permute-start | bytes 786440 | tf_op jit(solution)/shard_map/ppermute | solution.py:142
  9.9 0.0 collective-permute-start.12
  9.9 6.7 %collective-permute-done.8 = bf16[1,8,128,128]{3,2,1,0:T(8,128)(2,1)S(1)} collective-permute-done((bf16[1,8,128,128]{3,2,1,0:T(8,128)(2,1)S(1)}, bf16[1,8,128,128]{3,2,1,0:T(8,128)(2,1)S(1)}, u32[]{:S(2)}, u32[]{:S(2)}) %collective-permute-start.8) | collective-permute-done | bytes 262176 | tf_op jit(solution)/shard_map/ppermute | solution.py:147
  16.6 0.0 collective-permute-start.16
  16.6 0.0 copy-done
  16.6 1.0 %convolution_convert_fusion = bf16[2,128,1024]{2,1,0:T(8,128)(2,1)S(1)} fusion(bf16[2,128,1024]{2,1,0:T(8,128)(2,1)S(1)} %bitcast.60, s32[2,128]{1,0:T(2,128)} %param.11), kind=kOutput, calls=%fused_computation.3 | convolution fusion | flops 67403776 | bytes 1049600 | tf_op jit(solution)/shard_map/kpq,kqn->kpn/dot_general | solution.py:109
  17.7 0.0 collective-permute-done.7
  17.7 0.6 collective-permute-start.15
  18.3 1.8 %collective-permute-done.6 = bf16[1,8,128,128]{3,2,1,0:T(8,128)(2,1)S(1)} collective-permute-done((bf16[1,8,128,128]{3,2,1,0:T(8,128)(2,1)S(1)}, bf16[1,8,128,128]{3,2,1,0:T(8,128)(2,1)S(1)}, u32[]{:S(2)}, u32[]{:S(2)}) %collective-permute-start.6) | collective-permute-done | bytes 262176 | tf_op jit(solution)/shard_map/ppermute | solution.py:147
  20.0 0.0 collective-permute-start.14
  20.0 0.0 collective-permute-done.5
  20.1 0.5 collective-permute-start.13
  20.6 0.7 subtract_select_fusion
  21.3 0.1 stack.118
  21.4 0.0 collective-permute-done.12
  21.4 1.7 %collective-permute-start.2 = (bf16[256,1024]{1,0:T(8,128)(2,1)S(1)}, bf16[256,1024]{1,0:T(8,128)(2,1)}, u32[]{:S(2)}, u32[]{:S(2)}) collective-permute-start(bf16[256,1024]{1,0:T(8,128)(2,1)S(1)} %bitcast.66), channel_id=1, source_target_pairs={{0,16},{16,0},{32,48},{48,32},{64,80},{80,64},{96,112},{112,96},{1... | collective-permute-start | bytes 1572872 | tf_op jit(solution)/shard_map/ppermute | solution.py:118
  23.0 0.0 collective-permute-done.16
  23.0 1.9 %collective-permute-start.11 = (bf16[1,8,128,128]{3,2,1,0:T(8,128)(2,1)S(1)}, bf16[1,8,128,128]{3,2,1,0:T(8,128)(2,1)}, u32[]{:S(2)}, u32[]{:S(2)}) collective-permute-start(bf16[1,8,128,128]{3,2,1,0:T(8,128)(2,1)S(1)} %collective-permute-done.5), channel_id=1, source_target_pairs={{0,12},{1,13},{2,14},{3,15},{4,0},{5,1},{6,2},{7,3},{8,4},{9,5},{1... | collective-permute-start | bytes 786440 | tf_op jit(solution)/shard_map/ppermute | solution.py:147
  24.9 0.1 stack.135
  25.0 0.0 collective-permute-done.15
  25.1 2.8 %collective-permute-start.1 = (bf16[256,1024]{1,0:T(8,128)(2,1)S(1)}, bf16[256,1024]{1,0:T(8,128)(2,1)}, u32[]{:S(2)}, u32[]{:S(2)}) collective-permute-start(bf16[256,1024]{1,0:T(8,128)(2,1)S(1)} %bitcast.67), channel_id=1, source_target_pairs={{0,96},{16,112},{32,0},{48,16},{64,32},{80,48},{96,64},{112,80},{1... | collective-permute-start | bytes 1572872 | tf_op jit(solution)/shard_map/ppermute | solution.py:116
  27.9 0.0 collective-permute-done.14
  27.9 0.0 collective-permute-start
  27.9 0.0 collective-permute-done.13
  27.9 0.1 collective-permute-start.10
  28.0 0.1 select_reduce_fusion.1
  28.1 0.1 copy.9
  28.2 0.1 fusion.1
  28.3 7.9 %collective-permute-done.11 = bf16[1,8,128,128]{3,2,1,0:T(8,128)(2,1)} collective-permute-done((bf16[1,8,128,128]{3,2,1,0:T(8,128)(2,1)S(1)}, bf16[1,8,128,128]{3,2,1,0:T(8,128)(2,1)}, u32[]{:S(2)}, u32[]{:S(2)}) %collective-permute-start.11) | collective-permute-done | bytes 262176 | tf_op jit(solution)/shard_map/ppermute | solution.py:147
  36.1 0.0 collective-permute-start.9
  36.2 0.7 gather_fusion.1
  36.8 0.0 collective-permute-done.2.refs_3_
  36.8 2.8 %collective-permute-start.4 = (bf16[256,1024]{1,0:T(8,128)(2,1)}, bf16[256,1024]{1,0:T(8,128)(2,1)}, u32[]{:S(2)}, u32[]{:S(2)}) collective-permute-start(bf16[256,1024]{1,0:T(8,128)(2,1)} %collective-permute-done.2.refs_3_), channel_id=1, source_target_pairs={{0,96},{16,112},{32,0},{48,16},{64,32},{80,48},{96,64},{112,80},{1... | collective-permute-start | bytes 1572872 | tf_op jit(solution)/shard_map/ppermute | solution.py:116
  39.6 0.0 collective-permute-done.10
  39.7 0.0 collective-permute-start.3
  39.7 4.7 %collective-permute-done.9 = bf16[1,8,128,128]{3,2,1,0:T(8,128)(2,1)} collective-permute-done((bf16[1,8,128,128]{3,2,1,0:T(8,128)(2,1)S(1)}, bf16[1,8,128,128]{3,2,1,0:T(8,128)(2,1)}, u32[]{:S(2)}, u32[]{:S(2)}) %collective-permute-start.9) | collective-permute-done | bytes 262176 | tf_op jit(solution)/shard_map/ppermute | solution.py:147
  44.4 0.0 collective-permute-start.19
  44.4 0.0 collective-permute-done.1.refs_2_
  44.4 0.5 collective-permute-start.18
  44.9 0.0 collective-permute-done.refs_1_
  44.9 0.1 collective-permute-start.17
  45.0 0.1 select_reduce_fusion
  45.1 0.6 gather_fusion.2
  45.6 0.6 gather_fusion
  46.2 0.1 add_select_fusion
  46.3 0.0 collective-permute-done.19
  46.3 1.6 %collective-permute-start.20 = (bf16[256,1024]{1,0:T(8,128)(2,1)}, bf16[256,1024]{1,0:T(8,128)(2,1)S(1)}, u32[]{:S(2)}, u32[]{:S(2)}) collective-permute-start(bf16[256,1024]{1,0:T(8,128)(2,1)} %collective-permute-done.refs_1_), channel_id=1, source_target_pairs={{0,32},{16,48},{32,64},{48,80},{64,96},{80,112},{96,0},{112,16},{1... | collective-permute-start | bytes 1572872 | tf_op jit(solution)/shard_map/ppermute | solution.py:116
  47.8 2.3 %collective-permute-done.4.refs_5_ = bf16[256,1024]{1,0:T(8,128)(2,1)} collective-permute-done((bf16[256,1024]{1,0:T(8,128)(2,1)}, bf16[256,1024]{1,0:T(8,128)(2,1)}, u32[]{:S(2)}, u32[]{:S(2)}) %collective-permute-start.4) | collective-permute-done | bytes 524320 | tf_op jit(solution)/shard_map/ppermute | solution.py:116
  50.1 3.7 %collective-permute-start.21 = (bf16[256,1024]{1,0:T(8,128)(2,1)}, bf16[256,1024]{1,0:T(8,128)(2,1)S(1)}, u32[]{:S(2)}, u32[]{:S(2)}) collective-permute-start(bf16[256,1024]{1,0:T(8,128)(2,1)} %collective-permute-done.4.refs_5_), channel_id=1, source_target_pairs={{0,96},{16,112},{32,0},{48,16},{64,32},{80,48},{96,64},{112,80},{1... | collective-permute-start | bytes 1572872 | tf_op jit(solution)/shard_map/ppermute | solution.py:116
  53.8 0.0 collective-permute-done.18
  53.8 0.0 collective-permute-done.17
  53.8 2.2 %collective-permute-done.3.refs_4_ = bf16[256,1024]{1,0:T(8,128)(2,1)} collective-permute-done((bf16[256,1024]{1,0:T(8,128)(2,1)}, bf16[256,1024]{1,0:T(8,128)(2,1)}, u32[]{:S(2)}, u32[]{:S(2)}) %collective-permute-start.3) | collective-permute-done | bytes 524320 | tf_op jit(solution)/shard_map/ppermute | solution.py:116
  56.0 13.2 %shard_map.64.trailing_ref = f32[2048,1024]{1,0:T(8,128)} custom-call(s32[12,16]{1,0:T(8,128)S(1)} %bitcast.86, bf16[2048,1024]{1,0:T(8,128)(2,1)} %trailing_ref.1, bf16[256,1024]{1,0:T(8,128)(2,1)S(1)} %bitcast.69, bf16[256,1024]{1,0:T(8,128)(2,1)} %collective-permute-done.refs_1_, bf16[256,1024]{1,0:T(8,128)(2,1)} %collective-permute-done.1.refs_2_, ...), custom_call_target="tpu_custom_call" | custom-call | flops 6442450944 | bytes 19922944 | tf_op jit(solution)/shard_map/pallas_call | solution.py:77
  69.2 0.0 collective-permute-done.20.refs_0_
  69.2 0.0 collective-permute-done.21.refs_1_
  69.2 9.6 %shard_map.65 = bf16[2048,1024]{1,0:T(8,128)(2,1)} custom-call(s32[4,16]{1,0:T(4,128)S(1)} %slice.14.table_ref, f32[2048,1024]{1,0:T(8,128)} %shard_map.64.trailing_ref, bf16[256,1024]{1,0:T(8,128)(2,1)S(1)} %collective-permute-done.20.refs_0_, bf16[256,1024]{1,0:T(8,128)(2,1)S(1)} %collective-permute-done.21.refs_1_, ...), custom_call_target="tpu_custom_call" | custom-call | flops 2147483648 | bytes 17825792 | tf_op jit(solution)/shard_map/pallas_call | solution.py:77
  (4 shorter events, 0.0 us)
Async XLA Ops:
  0.0 16.6 %copy-start = (bf16[256,1024]{1,0:T(8,128)(2,1)S(1)}, bf16[256,1024]{1,0:T(8,128)(2,1)}, u32[]{:S(2)}) copy-start(bf16[256,1024]{1,0:T(8,128)(2,1)} %param.10) | copy-start | bytes 1572868
  1.2 15.4 %collective-permute-start.8 = (bf16[1,8,128,128]{3,2,1,0:T(8,128)(2,1)S(1)}, bf16[1,8,128,128]{3,2,1,0:T(8,128)(2,1)S(1)}, u32[]{:S(2)}, u32[]{:S(2)}) collective-permute-start(bf16[1,8,128,128]{3,2,1,0:T(8,128)(2,1)S(1)} %bitcast.61), channel_id=1, source_target_pairs={{0,12},{1,13},{2,14},{3,15},{4,0},{5,1},{6,2},{7,3},{8,4},{9,5},{1... | collective-permute-start | bytes 786440 | tf_op jit(solution)/shard_map/ppermute | solution.py:147
  5.4 12.2 %collective-permute-start.7 = (bf16[1,8,128,128]{3,2,1,0:T(8,128)(2,1)S(1)}, bf16[1,8,128,128]{3,2,1,0:T(8,128)(2,1)S(1)}, u32[]{:S(2)}, u32[]{:S(2)}) collective-permute-start(bf16[1,8,128,128]{3,2,1,0:T(8,128)(2,1)S(1)} %bitcast.62), channel_id=1, source_target_pairs={{0,8},{1,9},{2,10},{3,11},{4,12},{5,13},{6,14},{7,15},{8,0},{9,1},... | collective-permute-start | bytes 786440 | tf_op jit(solution)/shard_map/ppermute | solution.py:147
  5.4 14.6 %collective-permute-start.6 = (bf16[1,8,128,128]{3,2,1,0:T(8,128)(2,1)S(1)}, bf16[1,8,128,128]{3,2,1,0:T(8,128)(2,1)S(1)}, u32[]{:S(2)}, u32[]{:S(2)}) collective-permute-start(bf16[1,8,128,128]{3,2,1,0:T(8,128)(2,1)S(1)} %bitcast.63), channel_id=1, source_target_pairs={{0,4},{1,5},{2,6},{3,7},{4,8},{5,9},{6,10},{7,11},{8,12},{9,13},{1... | collective-permute-start | bytes 786440 | tf_op jit(solution)/shard_map/ppermute | solution.py:147
  6.7 13.3 %collective-permute-start.5 = (bf16[1,8,128,128]{3,2,1,0:T(8,128)(2,1)S(1)}, bf16[1,8,128,128]{3,2,1,0:T(8,128)(2,1)S(1)}, u32[]{:S(2)}, u32[]{:S(2)}) collective-permute-start(bf16[1,8,128,128]{3,2,1,0:T(8,128)(2,1)S(1)} %bitcast.64), channel_id=1, source_target_pairs={{0,2},{1,3},{2,0},{3,1},{4,6},{5,7},{6,4},{7,5},{8,10},{9,11},{10,... | collective-permute-start | bytes 786440 | tf_op jit(solution)/shard_map/ppermute | solution.py:142
  9.9 11.5 %collective-permute-start.12 = (bf16[1,8,128,128]{3,2,1,0:T(8,128)(2,1)S(1)}, bf16[1,8,128,128]{3,2,1,0:T(8,128)(2,1)S(1)}, u32[]{:S(2)}, u32[]{:S(2)}) collective-permute-start(bf16[1,8,128,128]{3,2,1,0:T(8,128)(2,1)S(1)} %bitcast.65), channel_id=1, source_target_pairs={{0,1},{1,0},{2,3},{3,2},{4,5},{5,4},{6,7},{7,6},{8,9},{9,8},{10,11... | collective-permute-start | bytes 786440 | tf_op jit(solution)/shard_map/ppermute | solution.py:151
  16.6 6.4 %collective-permute-start.16 = (bf16[1,8,128,128]{3,2,1,0:T(8,128)(2,1)S(1)}, bf16[1,8,128,128]{3,2,1,0:T(8,128)(2,1)S(1)}, u32[]{:S(2)}, u32[]{:S(2)}) collective-permute-start(bf16[1,8,128,128]{3,2,1,0:T(8,128)(2,1)S(1)} %collective-permute-done.8), channel_id=1, source_target_pairs={{0,1},{1,0},{2,3},{3,2},{4,5},{5,4},{6,7},{7,6},{8,9},{9,8},{10,11... | collective-permute-start | bytes 786440 | tf_op jit(solution)/shard_map/ppermute | solution.py:151
  17.7 7.4 %collective-permute-start.15 = (bf16[1,8,128,128]{3,2,1,0:T(8,128)(2,1)S(1)}, bf16[1,8,128,128]{3,2,1,0:T(8,128)(2,1)S(1)}, u32[]{:S(2)}, u32[]{:S(2)}) collective-permute-start(bf16[1,8,128,128]{3,2,1,0:T(8,128)(2,1)S(1)} %collective-permute-done.7), channel_id=1, source_target_pairs={{0,1},{1,0},{2,3},{3,2},{4,5},{5,4},{6,7},{7,6},{8,9},{9,8},{10,11... | collective-permute-start | bytes 786440 | tf_op jit(solution)/shard_map/ppermute | solution.py:151
  20.0 7.8 %collective-permute-start.14 = (bf16[1,8,128,128]{3,2,1,0:T(8,128)(2,1)S(1)}, bf16[1,8,128,128]{3,2,1,0:T(8,128)(2,1)S(1)}, u32[]{:S(2)}, u32[]{:S(2)}) collective-permute-start(bf16[1,8,128,128]{3,2,1,0:T(8,128)(2,1)S(1)} %collective-permute-done.6), channel_id=1, source_target_pairs={{0,1},{1,0},{2,3},{3,2},{4,5},{5,4},{6,7},{7,6},{8,9},{9,8},{10,11... | collective-permute-start | bytes 786440 | tf_op jit(solution)/shard_map/ppermute | solution.py:151
  20.1 7.8 %collective-permute-start.13 = (bf16[1,8,128,128]{3,2,1,0:T(8,128)(2,1)S(1)}, bf16[1,8,128,128]{3,2,1,0:T(8,128)(2,1)}, u32[]{:S(2)}, u32[]{:S(2)}) collective-permute-start(bf16[1,8,128,128]{3,2,1,0:T(8,128)(2,1)S(1)} %collective-permute-done.5), channel_id=1, source_target_pairs={{0,1},{1,0},{2,3},{3,2},{4,5},{5,4},{6,7},{7,6},{8,9},{9,8},{10,11... | collective-permute-start | bytes 786440 | tf_op jit(solution)/shard_map/ppermute | solution.py:151
  21.4 15.4 %collective-permute-start.2 = (bf16[256,1024]{1,0:T(8,128)(2,1)S(1)}, bf16[256,1024]{1,0:T(8,128)(2,1)}, u32[]{:S(2)}, u32[]{:S(2)}) collective-permute-start(bf16[256,1024]{1,0:T(8,128)(2,1)S(1)} %bitcast.66), channel_id=1, source_target_pairs={{0,16},{16,0},{32,48},{48,32},{64,80},{80,64},{96,112},{112,96},{1... | collective-permute-start | bytes 1572872 | tf_op jit(solution)/shard_map/ppermute | solution.py:118
  23.0 13.1 %collective-permute-start.11 = (bf16[1,8,128,128]{3,2,1,0:T(8,128)(2,1)S(1)}, bf16[1,8,128,128]{3,2,1,0:T(8,128)(2,1)}, u32[]{:S(2)}, u32[]{:S(2)}) collective-permute-start(bf16[1,8,128,128]{3,2,1,0:T(8,128)(2,1)S(1)} %collective-permute-done.5), channel_id=1, source_target_pairs={{0,12},{1,13},{2,14},{3,15},{4,0},{5,1},{6,2},{7,3},{8,4},{9,5},{1... | collective-permute-start | bytes 786440 | tf_op jit(solution)/shard_map/ppermute | solution.py:147
  25.1 19.3 %collective-permute-start.1 = (bf16[256,1024]{1,0:T(8,128)(2,1)S(1)}, bf16[256,1024]{1,0:T(8,128)(2,1)}, u32[]{:S(2)}, u32[]{:S(2)}) collective-permute-start(bf16[256,1024]{1,0:T(8,128)(2,1)S(1)} %bitcast.67), channel_id=1, source_target_pairs={{0,96},{16,112},{32,0},{48,16},{64,32},{80,48},{96,64},{112,80},{1... | collective-permute-start | bytes 1572872 | tf_op jit(solution)/shard_map/ppermute | solution.py:116
  27.9 17.0 %collective-permute-start = (bf16[256,1024]{1,0:T(8,128)(2,1)S(1)}, bf16[256,1024]{1,0:T(8,128)(2,1)}, u32[]{:S(2)}, u32[]{:S(2)}) collective-permute-start(bf16[256,1024]{1,0:T(8,128)(2,1)S(1)} %bitcast.68), channel_id=1, source_target_pairs={{0,32},{16,48},{32,64},{48,80},{64,96},{80,112},{96,0},{112,16},{1... | collective-permute-start | bytes 1572872 | tf_op jit(solution)/shard_map/ppermute | solution.py:116
  27.9 11.8 %collective-permute-start.10 = (bf16[1,8,128,128]{3,2,1,0:T(8,128)(2,1)S(1)}, bf16[1,8,128,128]{3,2,1,0:T(8,128)(2,1)}, u32[]{:S(2)}, u32[]{:S(2)}) collective-permute-start(bf16[1,8,128,128]{3,2,1,0:T(8,128)(2,1)S(1)} %collective-permute-done.5), channel_id=1, source_target_pairs={{0,8},{1,9},{2,10},{3,11},{4,12},{5,13},{6,14},{7,15},{8,0},{9,1},... | collective-permute-start | bytes 786440 | tf_op jit(solution)/shard_map/ppermute | solution.py:147
  36.1 8.2 %collective-permute-start.9 = (bf16[1,8,128,128]{3,2,1,0:T(8,128)(2,1)S(1)}, bf16[1,8,128,128]{3,2,1,0:T(8,128)(2,1)}, u32[]{:S(2)}, u32[]{:S(2)}) collective-permute-start(bf16[1,8,128,128]{3,2,1,0:T(8,128)(2,1)S(1)} %collective-permute-done.5), channel_id=1, source_target_pairs={{0,4},{1,5},{2,6},{3,7},{4,8},{5,9},{6,10},{7,11},{8,12},{9,13},{1... | collective-permute-start | bytes 786440 | tf_op jit(solution)/shard_map/ppermute | solution.py:147
  36.8 13.3 %collective-permute-start.4 = (bf16[256,1024]{1,0:T(8,128)(2,1)}, bf16[256,1024]{1,0:T(8,128)(2,1)}, u32[]{:S(2)}, u32[]{:S(2)}) collective-permute-start(bf16[256,1024]{1,0:T(8,128)(2,1)} %collective-permute-done.2.refs_3_), channel_id=1, source_target_pairs={{0,96},{16,112},{32,0},{48,16},{64,32},{80,48},{96,64},{112,80},{1... | collective-permute-start | bytes 1572872 | tf_op jit(solution)/shard_map/ppermute | solution.py:116
  39.7 16.3 %collective-permute-start.3 = (bf16[256,1024]{1,0:T(8,128)(2,1)}, bf16[256,1024]{1,0:T(8,128)(2,1)}, u32[]{:S(2)}, u32[]{:S(2)}) collective-permute-start(bf16[256,1024]{1,0:T(8,128)(2,1)} %collective-permute-done.2.refs_3_), channel_id=1, source_target_pairs={{0,32},{16,48},{32,64},{48,80},{64,96},{80,112},{96,0},{112,16},{1... | collective-permute-start | bytes 1572872 | tf_op jit(solution)/shard_map/ppermute | solution.py:116
  44.4 1.9 %collective-permute-start.19 = (bf16[1,8,128,128]{3,2,1,0:T(8,128)(2,1)}, bf16[1,8,128,128]{3,2,1,0:T(8,128)(2,1)}, u32[]{:S(2)}, u32[]{:S(2)}) collective-permute-start(bf16[1,8,128,128]{3,2,1,0:T(8,128)(2,1)} %collective-permute-done.11), channel_id=1, source_target_pairs={{0,1},{1,0},{2,3},{3,2},{4,5},{5,4},{6,7},{7,6},{8,9},{9,8},{10,11... | collective-permute-start | bytes 786440 | tf_op jit(solution)/shard_map/ppermute | solution.py:151
  44.4 9.4 %collective-permute-start.18 = (bf16[1,8,128,128]{3,2,1,0:T(8,128)(2,1)}, bf16[1,8,128,128]{3,2,1,0:T(8,128)(2,1)}, u32[]{:S(2)}, u32[]{:S(2)}) collective-permute-start(bf16[1,8,128,128]{3,2,1,0:T(8,128)(2,1)} %collective-permute-done.10), channel_id=1, source_target_pairs={{0,1},{1,0},{2,3},{3,2},{4,5},{5,4},{6,7},{7,6},{8,9},{9,8},{10,11... | collective-permute-start | bytes 786440 | tf_op jit(solution)/shard_map/ppermute | solution.py:151
  44.9 8.9 %collective-permute-start.17 = (bf16[1,8,128,128]{3,2,1,0:T(8,128)(2,1)}, bf16[1,8,128,128]{3,2,1,0:T(8,128)(2,1)}, u32[]{:S(2)}, u32[]{:S(2)}) collective-permute-start(bf16[1,8,128,128]{3,2,1,0:T(8,128)(2,1)} %collective-permute-done.9), channel_id=1, source_target_pairs={{0,1},{1,0},{2,3},{3,2},{4,5},{5,4},{6,7},{7,6},{8,9},{9,8},{10,11... | collective-permute-start | bytes 786440 | tf_op jit(solution)/shard_map/ppermute | solution.py:151
  46.3 22.9 %collective-permute-start.20 = (bf16[256,1024]{1,0:T(8,128)(2,1)}, bf16[256,1024]{1,0:T(8,128)(2,1)S(1)}, u32[]{:S(2)}, u32[]{:S(2)}) collective-permute-start(bf16[256,1024]{1,0:T(8,128)(2,1)} %collective-permute-done.refs_1_), channel_id=1, source_target_pairs={{0,32},{16,48},{32,64},{48,80},{64,96},{80,112},{96,0},{112,16},{1... | collective-permute-start | bytes 1572872 | tf_op jit(solution)/shard_map/ppermute | solution.py:116
  50.1 19.1 %collective-permute-start.21 = (bf16[256,1024]{1,0:T(8,128)(2,1)}, bf16[256,1024]{1,0:T(8,128)(2,1)S(1)}, u32[]{:S(2)}, u32[]{:S(2)}) collective-permute-start(bf16[256,1024]{1,0:T(8,128)(2,1)} %collective-permute-done.4.refs_5_), channel_id=1, source_target_pairs={{0,96},{16,112},{32,0},{48,16},{64,32},{80,48},{96,64},{112,80},{1... | collective-permute-start | bytes 1572872 | tf_op jit(solution)/shard_map/ppermute | solution.py:116
